TPU v7x, 32 devices: a whole 2x2x4 slice. The times are simulated.
32 devices in a mesh: ctx: 8 (over z, y), ch: 4 (over x, core).
Axes of the slice: x: 2, y: 2, z: 4, core: 2. Of those that a mesh axis runs over, the one named last changes fastest.
Arguments:
- projected: bfloat16 [3, 8192, 4096], P(None, 'ctx', 'ch'), may hold values from -6 to 6
- tap_weights: bfloat16 [3, 3, 4096], P(None, None, 'ch'), may hold values from -3.59375 to 3.59375
- pole_rates: float32 [16, 4096], P(None, 'ch'), may hold values from 1.2207031e-05 to 0.0625
- residues: float32 [16, 4096], P(None, 'ch'), may hold values from -1.4143862 to 1.4143862
- long_bias: float32 [4096], P('ch'), may hold values from -4 to 4
- out_weight: bfloat16 [4096, 4096], P(None, 'ch'), may hold values from -0.09375 to 0.09375
Outputs:
- mixed_out: bfloat16 [8192, 4096], P('ctx', 'ch')
All inputs are finite; a program needn't handle non-finite values.
Results may differ from a plain program's by a relative error of at most 0.012.
Values may be sent and summed in bfloat16 or wider, within the bound.
No kernel may reach another device: no remote copies, remote signals or barrier semaphores. Data moves between devices by JAX's collectives and lax.ppermute only.
A program may use at most 256 MiB of HBM per device.

v0:
```python
import jax
import jax.numpy as jnp
from jax import lax
from jax.sharding import PartitionSpec as P

BLOCK = 64


def shifted(value, axis, steps):
    count = lax.axis_size(axis)
    initial, last = (max(0, -steps), min(count, count - steps))
    return lax.ppermute(value, axis, [(source, source + steps) for source in range(initial, last)])


def make_tables(pole_rates, residues, block_size):
    lag_steps = jnp.arange(block_size, dtype=jnp.float32)
    powers = jnp.exp(-pole_rates[None, :, :] * lag_steps[:, None, None])
    kernel = jnp.sum(powers * residues[None, :, :], axis=1)
    offsets = (
        jnp.arange(block_size, dtype=jnp.int32)[:, None]
        - jnp.arange(block_size, dtype=jnp.int32)[None, :]
    )
    toeplitz = jnp.where(
        (offsets >= 0)[:, :, None], kernel[jnp.maximum(offsets, 0)], jnp.float32(0.0)
    )
    end_weights = powers[::-1]
    read_weights = powers * jnp.exp(-pole_rates)[None, :, :] * residues[None, :, :]
    block_decay = jnp.exp(-pole_rates * block_size)
    return (toeplitz, end_weights, read_weights, block_decay)


def combine(earlier, latter):
    return (earlier[0] * latter[0], latter[0] * earlier[1] + latter[1])


def channel_conv(rows_last, pole_rates, residues):
    highest = lax.Precision.HIGHEST
    channel_count = rows_last.shape[0]
    length = rows_last.shape[1]
    block_count = length // BLOCK
    pole_count = pole_rates.shape[0]
    toeplitz, end_weights, read_weights, block_decay = make_tables(pole_rates, residues, BLOCK)
    toeplitz_c = jnp.transpose(toeplitz, (2, 0, 1))
    blocks = rows_last.astype(jnp.float32).reshape(channel_count, block_count, BLOCK)
    inner_part = jnp.einsum("cij,cnj->cni", toeplitz_c, blocks, precision=highest)
    closing = jnp.einsum("jpc,cnj->ncp", end_weights, blocks, precision=highest)
    closing = closing.reshape(block_count, channel_count * pole_count)
    decay_row = jnp.transpose(block_decay).reshape(1, channel_count * pole_count)
    decays = jnp.broadcast_to(decay_row, closing.shape)
    _, states = lax.associative_scan(combine, (decays, closing), axis=0)
    before_state = jnp.concatenate([jnp.zeros_like(states[:1]), states[:-1]], 0)
    before_state = before_state.reshape(block_count, channel_count, pole_count)
    carried = jnp.einsum("ipc,ncp->cni", read_weights, before_state, precision=highest)
    return (inner_part + carried).reshape(channel_count, length)


def shards(projected, tap_weights, pole_rates, residues, long_bias, out_weight):
    row_count = projected.shape[1]
    rim_rows = tap_weights.shape[0] - 1
    prior_rows = shifted(projected[:, row_count - rim_rows :], "ctx", 1)
    extended = jnp.concatenate([prior_rows, projected], 1)
    featured = jnp.zeros(projected.shape, jnp.float32)
    for tap_index in range(rim_rows + 1):
        lead_row = rim_rows - tap_index
        featured = featured + tap_weights[tap_index].astype(jnp.float32)[:, None, :] * extended[
            :, lead_row : lead_row + row_count
        ].astype(jnp.float32)
    mixed_input = (featured[1] * featured[2]).astype(jnp.bfloat16)
    channel_major = jnp.transpose(mixed_input)
    spread = lax.all_to_all(channel_major, "ctx", split_axis=0, concat_axis=1, tiled=True)
    share_width = spread.shape[0]
    first_channel = lax.axis_index("ctx") * share_width
    rates_here = lax.dynamic_slice_in_dim(pole_rates, first_channel, share_width, 1)
    residues_here = lax.dynamic_slice_in_dim(residues, first_channel, share_width, 1)
    long_part = channel_conv(spread, rates_here, residues_here).astype(jnp.bfloat16)
    returned = lax.all_to_all(long_part, "ctx", split_axis=1, concat_axis=0, tiled=True)
    long_mix = jnp.transpose(returned)
    gated_mix = featured[0] * (
        long_mix.astype(jnp.float32) + long_bias[None, :] * mixed_input.astype(jnp.float32)
    )
    gated_mix = gated_mix.astype(jnp.bfloat16)
    mixed_out = jnp.dot(
        lax.all_gather(gated_mix, "ch", axis=1, tiled=True),
        out_weight,
        preferred_element_type=jnp.float32,
    )
    return mixed_out.astype(jnp.bfloat16)


def solution(mesh):
    in_specs = (
        P(None, "ctx", "ch"),
        P(None, None, "ch"),
        P(None, "ch"),
        P(None, "ch"),
        P("ch"),
        P(None, "ch"),
    )
    out_specs = P("ctx", "ch")
    return jax.shard_map(shards, mesh=mesh, in_specs=in_specs, out_specs=out_specs, check_vma=False)
```

profile of v0, /device:TPU:0, one launch (start us, length us, event | category | flops | bytes accessed | tf_op | source)
XLA Modules:
  0.0 405.2 jit_solution(4329657434524788336)
XLA Ops:
  7.4 4.9 %collective-permute-start = (bf16[3,2,1024]{2,1,0:T(2,128)(2,1)S(1)}, bf16[3,2,1024]{2,1,0:T(2,128)(2,1)S(1)}, u32[]{:S(2)}, u32[]{:S(2)}) collective-permute-start(bf16[3,2,1024]{2,1,0:T(2,128)(2,1)S(1)} %slice.176), channel_id=1, source_target_pairs={{0,4},{4,8},{8,12},{12,16},{16,20},{20,24},{24,28},{1,5},{5,9},{9,... | collective-permute-start | bytes 36872 | tf_op jit(solution)/shard_map/ppermute | solution.py:12
  13.0 8.7 %copy.43 = bf16[3,1024,1024]{1,2,0:T(8,128)(2,1)} copy(bf16[3,1024,1024]{2,1,0:T(8,128)(2,1)} %param.6) | data formatting | bytes 12582912 | tf_op args[0]
  22.1 15.7 %multiply_add_fusion = f32[3,1024,1024]{1,2,0:T(8,128)S(1)} fusion(bf16[3,1024,1024]{1,2,0:T(8,128)(2,1)} %copy.43, bf16[3,2,1024]{1,2,0:T(8,128)(2,1)S(1)} %copy.44, f32[3,1024]{1,0:T(4,128)S(1)} %get-tuple-element.12, f32[3,1024]{1,0:T(4,128)S(1)} %get-tuple-element.13, f32[3,1024]{1,0:T(4,128)S(1)} %get-tuple-element.11), kind=kLoop, calls=%fused_computation.1 | loop fusion | flops 44040192 | bytes 18923520 | tf_op jit(solution)/shard_map/add | solution.py:65
  37.8 4.5 %copy-done = f32[3,1024,1024]{1,2,0:T(8,128)} copy-done((f32[3,1024,1024]{1,2,0:T(8,128)}, f32[3,1024,1024]{1,2,0:T(8,128)S(1)}, u32[]{:S(2)}) %copy-start) | copy-done | bytes 12582936
  44.3 4.9 %all-to-all-start = ((bf16[8,128,1024]{2,1,0:T(8,128)(2,1)}), bf16[8,128,1024]{2,1,0:T(8,128)(2,1)}, u32[]{:S(2)}, u32[]{:S(2)}) async-start(bf16[8,128,1024]{2,1,0:T(8,128)(2,1)} %bitcast.6), calls=%async_computation | async-start | bytes 4194304 | tf_op jit(solution)/shard_map/all_to_all | solution.py:70
  53.5 10.8 %gather_fusion = f32[4096,128]{1,0:T(8,128)S(1)} fusion(f32[64,128]{1,0:T(8,128)S(1)} %copy.49, s32[4096]{0:T(1024)S(1)} %broadcast_clamp_fusion), kind=kCustom, calls=%fused_computation | custom fusion | bytes 4210688 | tf_op jit(solution)/shard_map/gather | solution.py:24
  64.3 4.6 %copy.50 = f32[64,64,128]{1,0,2:T(8,128)} copy(f32[64,64,128]{2,1,0:T(8,128)S(1)} %bitcast.56) | data formatting | bytes 4194304 | tf_op jit(solution)/shard_map/gather | solution.py:24
  70.8 26.5 %all-to-all-done = bf16[8,128,1024]{2,1,0:T(8,128)(2,1)} async-done(((bf16[8,128,1024]{2,1,0:T(8,128)(2,1)}), bf16[8,128,1024]{2,1,0:T(8,128)(2,1)}, u32[]{:S(2)}, u32[]{:S(2)}) %all-to-all-start) | async-done | bytes 2097184 | tf_op jit(solution)/shard_map/all_to_all | solution.py:70
  97.3 3.9 copy.46
  101.2 3.8 copy.51
  105.0 3.0 fusion.25
  108.0 20.3 %slice.187 = f32[64,2048]{0,1:T(8,128)} slice(f32[128,2048]{0,1:T(8,128)S(1)} %bitcast.52), slice={[0:127:2], [0:2048:1]} | slice | bytes 1048576 | tf_op jit(solution)/shard_map/slice | solution.py:50
  128.3 21.9 %slice.188 = f32[64,2048]{0,1:T(8,128)} slice(f32[128,2048]{0,1:T(8,128)S(1)} %bitcast.53), slice={[1:128:2], [0:2048:1]} | slice | bytes 1048576 | tf_op jit(solution)/shard_map/slice | solution.py:50
  150.2 2.4 copy.62
  152.5 2.4 copy.63
  154.9 2.1 multiply_add_fusion.1
  184.5 21.6 %slice.226 = f32[63,2048]{0,1:T(8,128)} slice(f32[128,2048]{0,1:T(8,128)S(1)} %bitcast.54), slice={[2:128:2], [0:2048:1]} | slice | bytes 1032192 | tf_op jit(solution)/shard_map/slice | solution.py:50
  220.8 2.7 pad.55
  225.6 4.6 %pad.116 = f32[128,2048]{1,0:T(8,128)} pad(f32[64,2048]{1,0:T(8,128)} %add.128, f32[]{:T(128)} %constant.5.clone.1), padding=1_0_1x0_0_0 | pad | bytes 1572868
  230.2 2.4 copy.64
  232.6 2.2 fusion.11
  237.2 2.1 pad.76
  239.3 2.3 slice_add_fusion.2
  243.5 4.2 %fusion.4 = f32[128,128,64]{1,2,0:T(8,128)S(1)} fusion(bf16[128,128,64]{1,2,0:T(8,128)(2,1)S(1)} %copy.51, f32[64,64,128]{1,0,2:T(8,128)} %copy.50, pred[64,64]{1,0:T(8,128)(4,1)S(1)} %copy-done.8), kind=kOutput, calls=%fused_computation.12 | convolution fusion | flops 805830656 | bytes 8392704 | tf_op jit(solution)/shard_map/cij,cnj->cni/dot_general | solution.py:45
  247.7 7.8 %add_convert_fusion = bf16[128,128,64]{1,2,0:T(8,128)(2,1)S(1)} fusion(f32[128,128,64]{1,2,0:T(8,128)S(1)} %fusion.4, f32[128,128,16]{0,2,1:T(8,128)S(1)} %bitcast.59, f32[16,128]{0,1:T(8,128)S(1)} %copy-done.6, f32[16,128]{0,1:T(8,128)S(1)} %copy-done.5, f32[16,128]{0,1:T(8,128)S(1)} %copy-done.3), kind=kOutput, calls=%fused_computation.15 | convolution fusion | flops 203816960 | bytes 7364608 | tf_op jit(solution)/shard_map/ipc,ncp->cni/dot_general | solution.py:53
  255.6 3.3 copy.60
  258.8 52.0 %all_to_all.26 = bf16[128,8,1024]{0,2,1:T(8,128)(2,1)S(1)} all-to-all(bf16[128,8,1024]{0,2,1:T(8,128)(2,1)} %bitcast.58), channel_id=1, replica_groups=mesh['ctx'=8,'ch'=4] {'ctx'}, dimensions={1} | all-to-all | bytes 4194304 | tf_op jit(solution)/shard_map/all_to_all | solution.py:76
  310.9 2.2 convert_bitcast_fusion
  313.1 5.4 %copy.61 = f32[8,128,1024]{2,1,0:T(8,128)} copy(f32[8,128,1024]{1,2,0:T(8,128)} %convert_bitcast_fusion) | data formatting | bytes 8388608 | tf_op jit(solution)/shard_map/convert_element_type | solution.py:79
  318.5 7.7 %fusion.3 = bf16[1024,1024]{0,1:T(8,128)(2,1)} fusion(f32[3,1024,1024]{1,2,0:T(8,128)} %copy-done, f32[8,128,1024]{2,1,0:T(8,128)} %copy.61, f32[1024]{0:T(1024)S(1)} %copy-done.9), kind=kLoop, calls=%fused_computation.10 | loop fusion | flops 7340032 | bytes 18878464 | tf_op jit(solution)/shard_map/convert_element_type | solution.py:81
  326.2 57.5 %all-gather.2.cloned.1.call-done = bf16[1024,4096]{0,1:T(8,128)(2,1)} async-done(((bf16[1024,1024]{0,1:T(8,128)(2,1)}), bf16[1024,4096]{0,1:T(8,128)(2,1)}) %all-gather.2.cloned.1.call-update) | async-done | bytes 8388624 | tf_op jit(solution)/shard_map/all_gather | solution.py:83
  383.7 14.7 %convolution_convert_fusion = bf16[1024,1024]{1,0:T(8,128)(2,1)} fusion(bf16[1024,4096]{0,1:T(8,128)(2,1)} %all-gather.2.cloned.1.call-done, bf16[4096,1024]{1,0:T(8,128)(2,1)} %param.11), kind=kOutput, calls=%fused_computation.19 | convolution fusion | flops 8590983168 | bytes 18874368 | tf_op jit(solution)/shard_map/dot_general | solution.py:82
  (99 shorter events, 58.7 us)
Async XLA Ops:
  7.4 14.3 %collective-permute-start = (bf16[3,2,1024]{2,1,0:T(2,128)(2,1)S(1)}, bf16[3,2,1024]{2,1,0:T(2,128)(2,1)S(1)}, u32[]{:S(2)}, u32[]{:S(2)}) collective-permute-start(bf16[3,2,1024]{2,1,0:T(2,128)(2,1)S(1)} %slice.176), channel_id=1, source_target_pairs={{0,4},{4,8},{8,12},{12,16},{16,20},{20,24},{24,28},{1,5},{5,9},{9,... | collective-permute-start | bytes 36872 | tf_op jit(solution)/shard_map/ppermute | solution.py:12
  37.8 4.5 %copy-start = (f32[3,1024,1024]{1,2,0:T(8,128)}, f32[3,1024,1024]{1,2,0:T(8,128)S(1)}, u32[]{:S(2)}) copy-start(f32[3,1024,1024]{1,2,0:T(8,128)S(1)} %multiply_add_fusion) | copy-start | bytes 37748740
  44.3 52.9 %all-to-all-start = ((bf16[8,128,1024]{2,1,0:T(8,128)(2,1)}), bf16[8,128,1024]{2,1,0:T(8,128)(2,1)}, u32[]{:S(2)}, u32[]{:S(2)}) async-start(bf16[8,128,1024]{2,1,0:T(8,128)(2,1)} %bitcast.6), calls=%async_computation | async-start | bytes 4194304 | tf_op jit(solution)/shard_map/all_to_all | solution.py:70
  49.2 334.5 %all-gather.2.cloned.1.call-start = ((), (), s32[]{:S(2)}) async-start(), calls=%async_computation.2 | async-start | bytes 10485760 | tf_op jit(solution)/shard_map/all_gather | solution.py:83
  50.1 3.4 copy-start.2
  50.2 3.3 copy-start.4
  70.8 89.6 %copy-start.7 = (f32[2048]{0:T(1024)}, f32[2048]{0:T(1024)S(1)}, u32[]{:S(2)}) copy-start(f32[2048]{0:T(1024)S(1)} %get-tuple-element.17) | copy-start | bytes 24580
  181.4 37.7 %slice-start = ((f32[64,2048]{1,0:T(8,128)}), f32[1,2048]{1,0:T(1,128)S(1)}, s32[]{:S(2)}) async-start(f32[64,2048]{1,0:T(8,128)} %multiply_add_fusion.1), calls=%async_computation.3 | async-start | bytes 16384 | tf_op jit(solution)/shard_map/slice | solution.py:50
  210.8 0.7 copy-start.1
  237.2 6.3 %copy-start.8 = (pred[64,64]{1,0:T(8,128)(4,1)S(1)}, pred[64,64]{1,0:T(8,128)(4,1)}, u32[]{:S(2)}) copy-start(pred[64,64]{1,0:T(8,128)(4,1)} %subtract_compare_fusion) | copy-start | bytes 12292
  243.5 4.2 %copy-start.3 = (f32[16,128]{0,1:T(8,128)S(1)}, f32[16,128]{0,1:T(8,128)}, u32[]{:S(2)}) copy-start(f32[16,128]{0,1:T(8,128)} %copy-done.2) | copy-start | bytes 24580
  243.5 4.2 %copy-start.5 = (f32[16,128]{0,1:T(8,128)S(1)}, f32[16,128]{0,1:T(8,128)}, u32[]{:S(2)}) copy-start(f32[16,128]{0,1:T(8,128)} %copy-done.4) | copy-start | bytes 24580
  243.5 4.2 %copy-start.6 = (f32[16,128]{0,1:T(8,128)S(1)}, f32[16,128]{0,1:T(8,128)}, u32[]{:S(2)}) copy-start(f32[16,128]{0,1:T(8,128)} %copy.59) | copy-start | bytes 24580
  313.1 5.4 %copy-start.9 = (f32[1024]{0:T(1024)S(1)}, f32[1024]{0:T(1024)}, u32[]{:S(2)}) copy-start(f32[1024]{0:T(1024)} %param.10) | copy-start | bytes 12292
Sparse Core Ops, SparseCore 0:
  326.3 57.3 all-gather.1
where the time goes:
time: 408 us; the launch traced here: 405 us
  local copies, waits for them, and re-layouts  157 us (38%)
  waiting for transfers between devices  84 us (21%)
  other arithmetic  59.2 us (15%)
  blocking collectives  52 us (13%)
  matrix products  29.6 us (7%)
  between operations  13.7 us (3%)
  starting transfers between devices  9.79 us (2%)
    slice x24, local copies, waits for them, and re-layouts, channel_conv(): _, states = lax.associative_scan(combine, (decays, closing), axis=0)  83.2 us
    all_gather x1, waiting for transfers between devices, shards(): lax.all_gather(gated_mix, 'ch', axis=1, tiled=True)  57.5 us
    all_to_all x1, blocking collectives, shards(): lax.all_to_all(long_part, 'ctx', split_axis=1, concat_axis=0, tiled=True)  52 us
    unnamed x26, local copies, waits for them, and re-layouts  27.2 us
    all_to_all x1, waiting for transfers between devices, shards(): lax.all_to_all(channel_major, 'ctx', split_axis=0, concat_axis=1, tiled=T...  26.5 us
    add x1, other arithmetic, shards(): featured + tap_weights[tap_index].astype(jnp.float32)[:, None, :] * exten...  15.7 us
    gather x2, local copies, waits for them, and re-layouts, make_tables(): kernel[jnp.maximum(offsets, 0)]  15.3 us
    dot_general x1, matrix products, shards(): jnp.dot(lax.all_gather(gated_mix, 'ch', axis=1, tiled=True), out_weight,...  14.7 us
  transfers between devices with their start and end apart: 3, of which 2 were waited for; matrix products, arithmetic and copies ran while one was open for 8% of the time, Pallas kernels for 0%

commit v1 on v0

--- a/solution.py
+++ b/solution.py
@@ -73,7 +73,10 @@
     rates_here = lax.dynamic_slice_in_dim(pole_rates, first_channel, share_width, 1)
     residues_here = lax.dynamic_slice_in_dim(residues, first_channel, share_width, 1)
     long_part = channel_conv(spread, rates_here, residues_here).astype(jnp.bfloat16)
-    returned = lax.all_to_all(long_part, "ctx", split_axis=1, concat_axis=0, tiled=True)
+    size = lax.axis_size("ctx")
+    pieces = jnp.stack(jnp.split(long_part, size, axis=1), axis=0)
+    pieces = lax.all_to_all(pieces, "ctx", split_axis=0, concat_axis=0)
+    returned = jnp.concatenate(pieces, axis=0)
     long_mix = jnp.transpose(returned)
     gated_mix = featured[0] * (
         long_mix.astype(jnp.float32) + long_bias[None, :] * mixed_input.astype(jnp.float32)

time: 408 us -> 405 us (level)
    unnamed x26 -> x33, local copies, waits for them, and re-layouts: 27.2 us -> 27.4 us
where the time goes in v1:
time: 405 us; the launch traced here: 402 us
  local copies, waits for them, and re-layouts  155 us (38%)
  waiting for transfers between devices  84 us (21%)
  other arithmetic  56.9 us (14%)
  blocking collectives  51.8 us (13%)
  matrix products  30.6 us (8%)
  between operations  13.8 us (3%)
  starting transfers between devices  9.79 us (2%)
    slice x24, local copies, waits for them, and re-layouts, channel_conv(): _, states = lax.associative_scan(combine, (decays, closing), axis=0)  83.2 us
    all_gather x1, waiting for transfers between devices, shards(): lax.all_gather(gated_mix, 'ch', axis=1, tiled=True)  57.5 us
    all_to_all x1, blocking collectives, shards(): pieces = lax.all_to_all(pieces, 'ctx', split_axis=0, concat_axis=0)  51.8 us
    unnamed x33, local copies, waits for them, and re-layouts  27.4 us
    all_to_all x1, waiting for transfers between devices, shards(): lax.all_to_all(channel_major, 'ctx', split_axis=0, concat_axis=1, tiled=T...  26.5 us
    add x1, other arithmetic, shards(): featured + tap_weights[tap_index].astype(jnp.float32)[:, None, :] * exten...  15.7 us
    gather x2, local copies, waits for them, and re-layouts, make_tables(): kernel[jnp.maximum(offsets, 0)]  15.3 us
    dot_general x1, matrix products, shards(): jnp.dot(lax.all_gather(gated_mix, 'ch', axis=1, tiled=True), out_weight,...  14.7 us
  transfers between devices with their start and end apart: 3, of which 2 were waited for; matrix products, arithmetic and copies ran while one was open for 8% of the time, Pallas kernels for 0%

profile of v1, /device:TPU:0, one launch (start us, length us, event | category | flops | bytes accessed | tf_op | source)
XLA Modules:
  0.0 402.3 jit_solution(9090954370749593440)
XLA Ops:
  7.4 4.9 %collective-permute-start = (bf16[3,2,1024]{2,1,0:T(2,128)(2,1)S(1)}, bf16[3,2,1024]{2,1,0:T(2,128)(2,1)S(1)}, u32[]{:S(2)}, u32[]{:S(2)}) collective-permute-start(bf16[3,2,1024]{2,1,0:T(2,128)(2,1)S(1)} %slice.176), channel_id=1, source_target_pairs={{0,4},{4,8},{8,12},{12,16},{16,20},{20,24},{24,28},{1,5},{5,9},{9,... | collective-permute-start | bytes 36872 | tf_op jit(solution)/shard_map/ppermute | solution.py:12
  13.0 8.7 %copy.54 = bf16[3,1024,1024]{1,2,0:T(8,128)(2,1)} copy(bf16[3,1024,1024]{2,1,0:T(8,128)(2,1)} %param.6) | data formatting | bytes 12582912 | tf_op args[0]
  22.1 15.7 %multiply_add_fusion = f32[3,1024,1024]{1,2,0:T(8,128)S(1)} fusion(bf16[3,1024,1024]{1,2,0:T(8,128)(2,1)} %copy.54, bf16[3,2,1024]{1,2,0:T(8,128)(2,1)S(1)} %copy.55, f32[3,1024]{1,0:T(4,128)S(1)} %get-tuple-element.12, f32[3,1024]{1,0:T(4,128)S(1)} %get-tuple-element.13, f32[3,1024]{1,0:T(4,128)S(1)} %get-tuple-element.11), kind=kLoop, calls=%fused_computation.1 | loop fusion | flops 44040192 | bytes 18923520 | tf_op jit(solution)/shard_map/add | solution.py:65
  37.8 4.5 %copy-done = f32[3,1024,1024]{1,2,0:T(8,128)} copy-done((f32[3,1024,1024]{1,2,0:T(8,128)}, f32[3,1024,1024]{1,2,0:T(8,128)S(1)}, u32[]{:S(2)}) %copy-start) | copy-done | bytes 12582936
  44.3 4.9 %all-to-all-start = ((bf16[8,128,1024]{2,1,0:T(8,128)(2,1)}), bf16[8,128,1024]{2,1,0:T(8,128)(2,1)}, u32[]{:S(2)}, u32[]{:S(2)}) async-start(bf16[8,128,1024]{2,1,0:T(8,128)(2,1)} %bitcast.6), calls=%async_computation | async-start | bytes 4194304 | tf_op jit(solution)/shard_map/all_to_all | solution.py:70
  53.5 10.8 %gather_fusion = f32[4096,128]{1,0:T(8,128)S(1)} fusion(f32[64,128]{1,0:T(8,128)S(1)} %copy.60, s32[4096]{0:T(1024)S(1)} %broadcast_clamp_fusion), kind=kCustom, calls=%fused_computation | custom fusion | bytes 4210688 | tf_op jit(solution)/shard_map/gather | solution.py:24
  64.3 4.6 %copy.61 = f32[64,64,128]{1,0,2:T(8,128)} copy(f32[64,64,128]{2,1,0:T(8,128)S(1)} %bitcast.86) | data formatting | bytes 4194304 | tf_op jit(solution)/shard_map/gather | solution.py:24
  70.8 26.5 %all-to-all-done = bf16[8,128,1024]{2,1,0:T(8,128)(2,1)} async-done(((bf16[8,128,1024]{2,1,0:T(8,128)(2,1)}), bf16[8,128,1024]{2,1,0:T(8,128)(2,1)}, u32[]{:S(2)}, u32[]{:S(2)}) %all-to-all-start) | async-done | bytes 2097184 | tf_op jit(solution)/shard_map/all_to_all | solution.py:70
  97.3 3.9 copy.57
  101.2 3.8 copy.62
  105.0 3.0 fusion.33
  108.0 20.3 %slice.187 = f32[64,2048]{0,1:T(8,128)} slice(f32[128,2048]{0,1:T(8,128)S(1)} %bitcast.82), slice={[0:127:2], [0:2048:1]} | slice | bytes 1048576 | tf_op jit(solution)/shard_map/slice | solution.py:50
  128.3 21.9 %slice.188 = f32[64,2048]{0,1:T(8,128)} slice(f32[128,2048]{0,1:T(8,128)S(1)} %bitcast.83), slice={[1:128:2], [0:2048:1]} | slice | bytes 1048576 | tf_op jit(solution)/shard_map/slice | solution.py:50
  150.2 2.4 copy.76
  152.5 2.4 copy.77
  154.9 2.1 multiply_add_fusion.1
  184.5 21.6 %slice.226 = f32[63,2048]{0,1:T(8,128)} slice(f32[128,2048]{0,1:T(8,128)S(1)} %bitcast.84), slice={[2:128:2], [0:2048:1]} | slice | bytes 1032192 | tf_op jit(solution)/shard_map/slice | solution.py:50
  220.8 2.7 pad.55
  223.5 2.1 add.128
  225.6 4.6 %pad.116 = f32[128,2048]{1,0:T(8,128)} pad(f32[64,2048]{1,0:T(8,128)} %add.128, f32[]{:T(128)} %constant.5.clone.1), padding=1_0_1x0_0_0 | pad | bytes 1572868
  230.2 2.4 copy.78
  232.6 2.2 fusion.11
  237.2 2.1 pad.76
  239.3 2.3 slice_add_fusion.2
  243.5 4.2 %fusion.4 = f32[128,128,64]{1,2,0:T(8,128)S(1)} fusion(bf16[128,128,64]{1,2,0:T(8,128)(2,1)S(1)} %copy.62, f32[64,64,128]{1,0,2:T(8,128)} %copy.61, pred[64,64]{1,0:T(8,128)(4,1)S(1)} %copy-done.8), kind=kOutput, calls=%fused_computation.12 | convolution fusion | flops 805830656 | bytes 8392704 | tf_op jit(solution)/shard_map/cij,cnj->cni/dot_general | solution.py:45
  247.7 8.8 %add_convert_fusion = bf16[128,128,64]{1,2,0:T(8,128)(2,1)} fusion(f32[128,128,64]{1,2,0:T(8,128)S(1)} %fusion.4, f32[128,128,16]{0,2,1:T(8,128)S(1)} %bitcast.96, f32[16,128]{0,1:T(8,128)S(1)} %copy-done.6, f32[16,128]{0,1:T(8,128)S(1)} %copy-done.5, f32[16,128]{0,1:T(8,128)S(1)} %copy-done.3), kind=kOutput, calls=%fused_computation.14 | convolution fusion | flops 203816960 | bytes 7364608 | tf_op jit(solution)/shard_map/ipc,ncp->cni/dot_general | solution.py:53
  256.5 3.8 copy.71
  260.7 51.8 %all_to_all.21 = bf16[8,128,1024]{1,2,0:T(8,128)(2,1)S(1)} all-to-all(bf16[8,128,1024]{1,2,0:T(8,128)(2,1)S(1)} %fusion.15), channel_id=1, replica_groups=mesh['ctx'=8,'ch'=4] {'ctx'}, dimensions={0} | all-to-all | bytes 4194304 | tf_op jit(solution)/shard_map/all_to_all | solution.py:78
  312.5 3.1 copy.74
  315.6 7.7 %fusion.3 = bf16[1024,1024]{0,1:T(8,128)(2,1)} fusion(f32[3,1024,1024]{1,2,0:T(8,128)} %copy-done, f32[8,128,1024]{2,1,0:T(8,128)} %copy.74, f32[1024]{0:T(1024)S(1)} %copy-done.9), kind=kLoop, calls=%fused_computation.10 | loop fusion | flops 7340032 | bytes 18878464 | tf_op jit(solution)/shard_map/convert_element_type | solution.py:84
  323.3 57.5 %all-gather.2.cloned.1.call-done = bf16[1024,4096]{0,1:T(8,128)(2,1)} async-done(((bf16[1024,1024]{0,1:T(8,128)(2,1)}), bf16[1024,4096]{0,1:T(8,128)(2,1)}) %all-gather.2.cloned.1.call-update) | async-done | bytes 8388624 | tf_op jit(solution)/shard_map/all_gather | solution.py:86
  380.8 14.7 %convolution_convert_fusion = bf16[1024,1024]{1,0:T(8,128)(2,1)} fusion(bf16[1024,4096]{0,1:T(8,128)(2,1)} %all-gather.2.cloned.1.call-done, bf16[4096,1024]{1,0:T(8,128)(2,1)} %param.11), kind=kOutput, calls=%fused_computation.18 | convolution fusion | flops 8590983168 | bytes 18874368 | tf_op jit(solution)/shard_map/dot_general | solution.py:85
  (106 shorter events, 56.9 us)
Async XLA Ops:
  7.4 14.3 %collective-permute-start = (bf16[3,2,1024]{2,1,0:T(2,128)(2,1)S(1)}, bf16[3,2,1024]{2,1,0:T(2,128)(2,1)S(1)}, u32[]{:S(2)}, u32[]{:S(2)}) collective-permute-start(bf16[3,2,1024]{2,1,0:T(2,128)(2,1)S(1)} %slice.176), channel_id=1, source_target_pairs={{0,4},{4,8},{8,12},{12,16},{16,20},{20,24},{24,28},{1,5},{5,9},{9,... | collective-permute-start | bytes 36872 | tf_op jit(solution)/shard_map/ppermute | solution.py:12
  37.8 4.5 %copy-start = (f32[3,1024,1024]{1,2,0:T(8,128)}, f32[3,1024,1024]{1,2,0:T(8,128)S(1)}, u32[]{:S(2)}) copy-start(f32[3,1024,1024]{1,2,0:T(8,128)S(1)} %multiply_add_fusion) | copy-start | bytes 37748740
  44.3 52.9 %all-to-all-start = ((bf16[8,128,1024]{2,1,0:T(8,128)(2,1)}), bf16[8,128,1024]{2,1,0:T(8,128)(2,1)}, u32[]{:S(2)}, u32[]{:S(2)}) async-start(bf16[8,128,1024]{2,1,0:T(8,128)(2,1)} %bitcast.6), calls=%async_computation | async-start | bytes 4194304 | tf_op jit(solution)/shard_map/all_to_all | solution.py:70
  49.2 331.6 %all-gather.2.cloned.1.call-start = ((), (), s32[]{:S(2)}) async-start(), calls=%async_computation.2 | async-start | bytes 10485760 | tf_op jit(solution)/shard_map/all_gather | solution.py:86
  50.1 3.4 copy-start.2
  50.2 3.3 copy-start.4
  70.8 89.6 %copy-start.7 = (f32[2048]{0:T(1024)}, f32[2048]{0:T(1024)S(1)}, u32[]{:S(2)}) copy-start(f32[2048]{0:T(1024)S(1)} %get-tuple-element.17) | copy-start | bytes 24580
  181.4 37.7 %slice-start = ((f32[64,2048]{1,0:T(8,128)}), f32[1,2048]{1,0:T(1,128)S(1)}, s32[]{:S(2)}) async-start(f32[64,2048]{1,0:T(8,128)} %multiply_add_fusion.1), calls=%async_computation.3 | async-start | bytes 16384 | tf_op jit(solution)/shard_map/slice | solution.py:50
  210.8 0.7 copy-start.1
  237.2 6.3 %copy-start.8 = (pred[64,64]{1,0:T(8,128)(4,1)S(1)}, pred[64,64]{1,0:T(8,128)(4,1)}, u32[]{:S(2)}) copy-start(pred[64,64]{1,0:T(8,128)(4,1)} %subtract_compare_fusion) | copy-start | bytes 12292
  243.5 4.2 %copy-start.3 = (f32[16,128]{0,1:T(8,128)S(1)}, f32[16,128]{0,1:T(8,128)}, u32[]{:S(2)}) copy-start(f32[16,128]{0,1:T(8,128)} %copy-done.2) | copy-start | bytes 24580
  243.5 4.2 %copy-start.5 = (f32[16,128]{0,1:T(8,128)S(1)}, f32[16,128]{0,1:T(8,128)}, u32[]{:S(2)}) copy-start(f32[16,128]{0,1:T(8,128)} %copy-done.4) | copy-start | bytes 24580
  243.5 4.2 %copy-start.6 = (f32[16,128]{0,1:T(8,128)S(1)}, f32[16,128]{0,1:T(8,128)}, u32[]{:S(2)}) copy-start(f32[16,128]{0,1:T(8,128)} %copy.70) | copy-start | bytes 24580
  312.5 3.1 copy-start.9
Sparse Core Ops, SparseCore 0:
  323.4 57.3 all-gather.1
